TPU v7x, 256 devices: a whole 4x4x8 slice. The times are simulated.
256 devices in a mesh: dp: 4 (over y), seq: 16 (over z, core), tensor: 4 (over x).
Axes of the slice: x: 4, y: 4, z: 8, core: 2. Of those that a mesh axis runs over, the one named last changes fastest.
Arguments:
- queries: bfloat16 [16384, 8192], P(('dp', 'seq'), 'tensor'), parts along dimension 0, may hold values from -110 to 110
- keys_values: bfloat16 [16384, 2, 1024], P(('dp', 'seq'), None, 'tensor'), parts along dimension 0, may hold values from -4.5 to 4.5
- out_weight: bfloat16 [8192, 8192], P('tensor', 'seq'), may hold values from -0.1875 to 0.1875
- residual: bfloat16 [16384, 8192], P(('dp', 'tensor'), 'seq'), parts along dimension 0, may hold values from -3 to 3
- segments: int32 [16384], P('dp'), parts along dimension 0, may hold values from 0 to 3, never falling along the last dimension, each value on 1 to 2048 neighbouring positions
Outputs:
- layer_out: bfloat16 [16384, 8192], P(('dp', 'tensor'), 'seq'), parts along dimension 0
There are 4 independent parts, one for each index of `dp`. A program takes and returns all parts, laid end to end along the dimension named above; an argument that names none is the same for every part. Nothing has to cross between parts.
Inputs may be any that keep to these rules, and one draw needn't show every extreme that they name: `segments`: segment numbers never fall along the tokens.
All inputs are finite; a program needn't handle non-finite values.
Results may differ from a plain program's by a relative error of at most 0.0085.
Values may be sent and summed in bfloat16 or wider, within the bound.
No kernel may reach another device: no remote copies, remote signals or barrier semaphores. Data moves between devices by JAX's collectives and lax.ppermute only.
A program may use at most 128 MiB of HBM per device.

v0:
```python
import jax
import jax.numpy as jnp
import numpy as np
from jax import lax
from jax.sharding import PartitionSpec as P

H = 64
KVH = 8
HD = 128
L = 4096
CHUNKS = 4


def attend_rows(query_head, key_head, value_head, doc_ids, first_row, rows):
    key_end = first_row + rows
    query_block = query_head[first_row:key_end]
    raw_scores = jnp.einsum(
        "qd,kd->qk", query_block, key_head[:key_end], preferred_element_type=jnp.float32
    ) * HD ** (-0.5)
    query_pos = first_row + jnp.arange(rows)[:, None]
    key_pos = jnp.arange(key_end)[None, :]
    same_doc = doc_ids[first_row:key_end, None] == doc_ids[None, :key_end]
    allowed = (key_pos <= query_pos) & same_doc
    masked = jnp.where(allowed, raw_scores, -1e30)
    highest = jnp.max(masked, axis=-1, keepdims=True)
    exponents = jnp.where(allowed, jnp.exp(masked - highest), 0.0)
    weights = (exponents / jnp.sum(exponents, axis=-1, keepdims=True)).astype(jnp.bfloat16)
    blended = jnp.einsum(
        "qk,kd->qd", weights, value_head[:key_end], preferred_element_type=jnp.float32
    )
    return blended.astype(jnp.bfloat16)


def on_device(queries, keys_values, out_weight, residual, segments):
    n_seq = lax.axis_size("seq")
    n_ten = lax.axis_size("tensor")
    seq_idx = lax.axis_index("seq")
    tok_dev = queries.shape[0]
    heads_ten = queries.shape[1] // HD
    heads_dev = heads_ten // n_seq
    assert heads_dev == 1
    group_size = H // KVH
    query_slab = queries.reshape(tok_dev, 1, heads_ten * HD)
    query_all = lax.all_to_all(query_slab, "seq", split_axis=2, concat_axis=0, tiled=True)
    query_head = query_all.reshape(query_all.shape[0], HD)
    rows_all = query_head.shape[0]
    assert rows_all == L
    pair_all = lax.all_gather(keys_values, "seq", axis=0, tiled=True)
    kv_local = seq_idx // group_size
    pair_head = lax.dynamic_slice_in_dim(pair_all, kv_local * HD, HD, axis=2)
    key_head = pair_head[:, 0, :]
    value_head = pair_head[:, 1, :]
    doc_ids = segments
    out_rows = rows_all // n_ten
    block_rows = out_rows // CHUNKS
    pieces = []
    for chunk in range(CHUNKS):
        blocks = [
            attend_rows(
                query_head,
                key_head,
                value_head,
                doc_ids,
                part * out_rows + chunk * block_rows,
                block_rows,
            )
            for part in range(n_ten)
        ]
        chunk_heads = jnp.concatenate(blocks, axis=0)
        gathered = lax.all_gather(chunk_heads, "seq", axis=1, tiled=True)
        projected = jnp.dot(gathered, out_weight, preferred_element_type=jnp.float32)
        pieces.append(lax.psum_scatter(projected, "tensor", scatter_dimension=0, tiled=True))
    summed = jnp.concatenate(pieces, axis=0)
    return (residual.astype(jnp.float32) + summed).astype(jnp.bfloat16)


def solution(mesh):
    placed = (
        P(("dp", "seq"), "tensor"),
        P(("dp", "seq"), None, "tensor"),
        P("tensor", "seq"),
        P(("dp", "tensor"), "seq"),
        P("dp"),
    )
    return jax.shard_map(
        on_device, mesh=mesh, in_specs=placed, out_specs=P(("dp", "tensor"), "seq"), check_vma=False
    )
```

profile of v0, /device:TPU:1, one launch (start us, length us, event | category | flops | bytes accessed | tf_op | source)
XLA Modules:
  0.0 436.0 jit_solution(1249033622516324133)
XLA Ops:
  6.5 1.8 copy.43
  8.4 5.9 %copy.44 = bf16[256,1,2048]{0,1,2:T(2,128)(2,1)} copy(bf16[256,1,2048]{2,0,1:T(8,128)(2,1)} %bitcast.316) | data formatting | bytes 2097152 | tf_op jit(solution)/shard_map/reshape | solution.py:43
  14.8 11.6 %reduce = bf16[2048,256]{1,0:T(8,128)(2,1)S(1)} reduce(bf16[2048,1,256]{2,1,0:T(2,128)(2,1)} %bitcast.306, bf16[]{:T(256)} %broadcast.172), dimensions={1}, to_apply=%bitcast.228.reduce_sub_computation | reduce | bytes 2097154
  26.5 1.1 reshape.191
  27.6 10.0 %all-to-all-start = ((bf16[16,2,16384]{2,1,0:T(2,128)(2,1)}), bf16[16,2,16384]{2,1,0:T(2,128)(2,1)S(1)}, u32[]{:S(2)}, u32[]{:S(2)}) async-start(bf16[16,2,16384]{2,1,0:T(2,128)(2,1)} %reshape.191), calls=%async_computation | async-start | bytes 2097152 | tf_op jit(solution)/shard_map/all_to_all | solution.py:44
  38.3 34.3 %all-to-all-done = bf16[16,2,16384]{2,1,0:T(2,128)(2,1)S(1)} async-done(((bf16[16,2,16384]{2,1,0:T(2,128)(2,1)}), bf16[16,2,16384]{2,1,0:T(2,128)(2,1)S(1)}, u32[]{:S(2)}, u32[]{:S(2)}) %all-to-all-start) | async-done | bytes 1048608 | tf_op jit(solution)/shard_map/all_to_all | solution.py:44
  72.5 3.5 reshape.192
  76.0 1.8 copy.61
  77.8 3.2 fusion.130
  81.0 1.9 fusion.30
  83.1 0.9 fusion.131
  84.0 1.4 fusion.39
  85.5 0.6 fusion.132
  86.1 0.7 fusion.52
  87.6 2.3 fusion.65
  89.8 1.7 fusion.69
  91.6 1.1 convolution_convert_fusion.1
  92.7 0.6 convolution_convert_fusion.2
  93.3 0.7 pad_maximum_fusion.3
  94.3 1.3 fusion.137
  95.9 1.6 convolution_convert_fusion.4
  97.9 0.6 fusion.136
  98.5 1.0 fusion.59
  99.4 0.8 fusion.135
  100.3 1.3 fusion.41
  101.6 1.1 fusion.134
  102.7 1.8 fusion.32
  104.5 1.0 convolution_convert_fusion.3
  105.5 1.6 fusion.68
  107.1 2.2 fusion.64
  109.3 0.7 pad_maximum_fusion.2
  110.4 1.3 fusion.141
  111.9 1.5 fusion.140
  114.4 0.8 fusion.139
  115.2 1.2 fusion.45
  116.4 1.0 fusion.138
  117.4 0.9 convolution_convert_fusion
  118.3 1.8 fusion.33
  120.1 1.4 fusion.67
  121.4 2.0 fusion.63
  123.5 0.7 pad_maximum_fusion.1
  124.6 1.2 fusion.145
  125.9 1.4 fusion.144
  128.1 0.7 fusion.143
  128.8 1.1 fusion.48
  129.9 1.0 fusion.142
  130.9 0.7 convolution_convert_fusion.6
  131.6 1.6 fusion.35
  133.3 1.3 fusion.66
  134.6 1.9 fusion.70
  136.5 0.7 pad_maximum_fusion
  137.3 4.7 %all-gather.14.cloned.1.call-done = bf16[1024,2048]{1,0:T(8,128)(2,1)} async-done(((bf16[1024,128]{1,0:T(8,128)(2,1)}), bf16[1024,2048]{1,0:T(8,128)(2,1)}) %all-gather.14.cloned.1.call-update) | async-done | bytes 4194320 | tf_op jit(solution)/shard_map/all_gather | solution.py:70
  142.0 5.9 %fusion.149 = f32[1024,512]{1,0:T(8,128)} fusion(bf16[1024,2048]{1,0:T(8,128)(2,1)} %all-gather.14.cloned.1.call-done, bf16[2048,512]{1,0:T(8,128)(2,1)S(1)} %copy-done), kind=kOutput, calls=%fused_computation.289 | convolution fusion | flops 2147483648 | bytes 8388608 | tf_op jit(solution)/shard_map/dot_general | solution.py:71
  147.9 43.5 %all-gather.12.cloned.1.call-done = bf16[1024,2048]{1,0:T(8,128)(2,1)} async-done(((bf16[1024,128]{1,0:T(8,128)(2,1)}), bf16[1024,2048]{1,0:T(8,128)(2,1)}) %all-gather.12.cloned.1.call-update) | async-done | bytes 4194320 | tf_op jit(solution)/shard_map/all_gather | solution.py:70
  191.5 5.9 %fusion.148 = f32[1024,512]{1,0:T(8,128)} fusion(bf16[1024,2048]{1,0:T(8,128)(2,1)} %all-gather.12.cloned.1.call-done, bf16[2048,512]{1,0:T(8,128)(2,1)S(1)} %copy-done), kind=kOutput, calls=%fused_computation.288 | convolution fusion | flops 2147483648 | bytes 8388608 | tf_op jit(solution)/shard_map/dot_general | solution.py:71
  197.7 43.0 %all-gather.10.cloned.1.call-done = bf16[1024,2048]{1,0:T(8,128)(2,1)} async-done(((bf16[1024,128]{1,0:T(8,128)(2,1)}), bf16[1024,2048]{1,0:T(8,128)(2,1)}) %all-gather.10.cloned.1.call-update) | async-done | bytes 4194320 | tf_op jit(solution)/shard_map/all_gather | solution.py:70
  240.7 5.8 %fusion.147 = f32[1024,512]{1,0:T(8,128)} fusion(bf16[1024,2048]{1,0:T(8,128)(2,1)} %all-gather.10.cloned.1.call-done, bf16[2048,512]{1,0:T(8,128)(2,1)S(1)} %copy-done), kind=kOutput, calls=%fused_computation.287 | convolution fusion | flops 2147483648 | bytes 8388608 | tf_op jit(solution)/shard_map/dot_general | solution.py:71
  246.6 43.3 %all-gather.8.cloned.1.call-done = bf16[1024,2048]{1,0:T(8,128)(2,1)} async-done(((bf16[1024,128]{1,0:T(8,128)(2,1)}), bf16[1024,2048]{1,0:T(8,128)(2,1)}) %all-gather.8.cloned.1.call-update) | async-done | bytes 4194320 | tf_op jit(solution)/shard_map/all_gather | solution.py:70
  289.9 5.8 %fusion.146 = f32[1024,512]{1,0:T(8,128)} fusion(bf16[1024,2048]{1,0:T(8,128)(2,1)} %all-gather.8.cloned.1.call-done, bf16[2048,512]{1,0:T(8,128)(2,1)S(1)} %copy-done), kind=kOutput, calls=%fused_computation.286 | convolution fusion | flops 2147483648 | bytes 8388608 | tf_op jit(solution)/shard_map/dot_general | solution.py:71
  295.8 26.6 %reduce-scatter.11.cloned.1.call-done = f32[256,512]{1,0:T(8,128)} async-done(((f32[1024,512]{1,0:T(8,128)}), f32[256,512]{1,0:T(8,128)}) %reduce-scatter.11.cloned.1.call-update) | async-done | bytes 524304 | tf_op jit(solution)/shard_map/reduce_scatter | solution.py:72
  322.4 34.6 %reduce-scatter.9.cloned.1.call-done = f32[256,512]{1,0:T(8,128)} async-done(((f32[1024,512]{1,0:T(8,128)}), f32[256,512]{1,0:T(8,128)}) %reduce-scatter.9.cloned.1.call-update) | async-done | bytes 524304 | tf_op jit(solution)/shard_map/reduce_scatter | solution.py:72
  357.0 34.6 %reduce-scatter.7.cloned.1.call-done = f32[256,512]{1,0:T(8,128)} async-done(((f32[1024,512]{1,0:T(8,128)}), f32[256,512]{1,0:T(8,128)}) %reduce-scatter.7.cloned.1.call-update) | async-done | bytes 524304 | tf_op jit(solution)/shard_map/reduce_scatter | solution.py:72
  391.6 34.6 %reduce-scatter.5.cloned.1.call-done = f32[256,512]{1,0:T(8,128)} async-done(((f32[1024,512]{1,0:T(8,128)}), f32[256,512]{1,0:T(8,128)}) %reduce-scatter.5.cloned.1.call-update) | async-done | bytes 524304 | tf_op jit(solution)/shard_map/reduce_scatter | solution.py:72
  426.2 2.8 fusion.36
  (69 shorter events, 6.2 us)
Async XLA Ops:
  6.5 135.5 %copy-start = (bf16[2048,512]{1,0:T(8,128)(2,1)S(1)}, bf16[2048,512]{1,0:T(8,128)(2,1)}, u32[]{:S(2)}) copy-start(bf16[2048,512]{1,0:T(8,128)(2,1)} %param.7) | copy-start | bytes 6291460
  6.5 71.3 %all-gather.6.cloned.1.call-start = ((), (), s32[]{:S(2)}) async-start(), calls=%async_computation.5 | async-start | bytes 4456448 | tf_op jit(solution)/shard_map/all_gather | solution.py:48
  26.5 11.7 %copy-start.1 = (s32[4096]{0:T(1024)S(1)}, s32[4096]{0:T(1024)}, u32[]{:S(2)}) copy-start(s32[4096]{0:T(1024)} %param.9) | copy-start | bytes 49156
  27.6 44.9 %all-to-all-start = ((bf16[16,2,16384]{2,1,0:T(2,128)(2,1)}), bf16[16,2,16384]{2,1,0:T(2,128)(2,1)S(1)}, u32[]{:S(2)}, u32[]{:S(2)}) async-start(bf16[16,2,16384]{2,1,0:T(2,128)(2,1)} %reshape.191), calls=%async_computation | async-start | bytes 2097152 | tf_op jit(solution)/shard_map/all_to_all | solution.py:44
  37.6 104.4 %all-gather.14.cloned.1.call-start = ((), (), s32[]{:S(2)}) async-start(), calls=%async_computation.12 | async-start | bytes 4456448 | tf_op jit(solution)/shard_map/all_gather | solution.py:70
  81.0 2.2 copy-start.3
  94.0 97.5 %all-gather.12.cloned.1.call-start = ((), (), s32[]{:S(2)}) async-start(), calls=%async_computation.10 | async-start | bytes 4456448 | tf_op jit(solution)/shard_map/all_gather | solution.py:70
  95.6 2.3 copy-start.4
  110.0 130.7 %all-gather.10.cloned.1.call-start = ((), (), s32[]{:S(2)}) async-start(), calls=%async_computation.8 | async-start | bytes 4456448 | tf_op jit(solution)/shard_map/all_gather | solution.py:70
  110.4 3.6 copy-start.5
  124.2 165.7 %all-gather.8.cloned.1.call-start = ((), (), s32[]{:S(2)}) async-start(), calls=%async_computation.6 | async-start | bytes 4456448 | tf_op jit(solution)/shard_map/all_gather | solution.py:70
  124.5 3.2 copy-start.6
  137.2 185.1 %reduce-scatter.11.cloned.1.call-start = ((), (), s32[]{:S(2)}) async-start(), calls=%async_computation.13 | async-start | bytes 2621440 | tf_op jit(solution)/shard_map/reduce_scatter | solution.py:72
  147.9 209.1 %reduce-scatter.9.cloned.1.call-start = ((), (), s32[]{:S(2)}) async-start(), calls=%async_computation.11 | async-start | bytes 2621440 | tf_op jit(solution)/shard_map/reduce_scatter | solution.py:72
  197.4 194.2 %reduce-scatter.7.cloned.1.call-start = ((), (), s32[]{:S(2)}) async-start(), calls=%async_computation.9 | async-start | bytes 2621440 | tf_op jit(solution)/shard_map/reduce_scatter | solution.py:72
  246.6 179.6 %copy-start.2 = (bf16[1024,512]{1,0:T(8,128)(2,1)S(1)}, bf16[1024,512]{1,0:T(8,128)(2,1)}, u32[]{:S(2)}) copy-start(bf16[1024,512]{1,0:T(8,128)(2,1)} %param.8) | copy-start | bytes 3145732
  246.6 179.6 %reduce-scatter.5.cloned.1.call-start = ((), (), s32[]{:S(2)}) async-start(), calls=%async_computation.7 | async-start | bytes 2621440 | tf_op jit(solution)/shard_map/reduce_scatter | solution.py:72
Sparse Core Ops, SparseCore 0:
  9.2 64.9 all-gather.5
  94.2 47.7 all-gather.13
  143.8 47.6 all-gather.11
  193.1 47.5 all-gather.9
  242.3 47.5 all-gather.7
  292.3 30.0 reduce-scatter.10
  324.9 31.9 reduce-scatter.8
  359.5 31.9 reduce-scatter.6
  394.1 32.0 reduce-scatter.4
where the time goes:
time: 440 us; the launch traced here: 436 us
  waiting for transfers between devices  299 us (68%)
  matrix products  62.2 us (14%)
  other arithmetic  33.2 us (8%)
  local copies, waits for them, and re-layouts  15.3 us (3%)
  between operations  14.2 us (3%)
  starting transfers between devices  11.8 us (3%)
    all_gather x4, waiting for transfers between devices, on_device(): gathered = lax.all_gather(chunk_heads, 'seq', axis=1, tiled=True)  135 us
    reduce_scatter x4, waiting for transfers between devices, on_device(): lax.psum_scatter(projected, 'tensor', scatter_dimension=0, tiled=True)  130 us
    all_to_all x1, waiting for transfers between devices, on_device(): lax.all_to_all(query_slab, 'seq', split_axis=2, concat_axis=0, tiled=True)  34.3 us
    dot_general x4, matrix products, on_device(): jnp.dot(gathered, out_weight, preferred_element_type=jnp.float32)  23.4 us
    dot_general x16, matrix products, attend_rows(): jnp.einsum('qk,kd->qd', weights, value_head[:key_end], preferred_element_...  21 us
    dot_general x16, matrix products, attend_rows(): jnp.einsum('qd,kd->qk', query_block, key_head[:key_end], preferred_elemen...  17.8 us
    reduce_sum x16, other arithmetic, attend_rows(): jnp.sum(exponents, axis=-1, keepdims=True)  15.8 us
    unnamed x1, other arithmetic  11.6 us
  transfers between devices with their start and end apart: 10, of which 9 were waited for; matrix products, arithmetic and copies ran while one was open for 21% of the time, Pallas kernels for 0%

commit v1 on v0

--- a/solution.py
+++ b/solution.py
@@ -9,6 +9,28 @@
 HD = 128
 L = 4096
 CHUNKS = 4
+
+
+def in_order(tiles, dim):
+    tiles = jnp.moveaxis(tiles, 0, dim)
+    dims = tiles.shape
+    return tiles.reshape(*dims[:dim], dims[dim] * dims[dim + 1], *dims[dim + 2 :])
+
+
+def gather_around(x, axis, dim):
+    count = lax.axis_size(axis)
+    pairs = [(i, (i + 1) % count) for i in range(count)]
+    back = [(b, a) for a, b in pairs]
+    lower, upper = ([], [])
+    for step in range(count - 1):
+        if step % 2 == 0:
+            lower.append(lax.ppermute(lower[-1] if lower else x, axis, pairs))
+        else:
+            upper.append(lax.ppermute(upper[-1] if upper else x, axis, back))
+    parts = jnp.stack([*lower[::-1], x, *upper])
+    shift = lax.axis_index(axis) - len(lower)
+    parts = parts[(jnp.arange(count) - shift) % count]
+    return in_order(parts, dim)
 
 
 def attend_rows(query_head, key_head, value_head, doc_ids, first_row, rows):
@@ -67,7 +89,7 @@
             for part in range(n_ten)
         ]
         chunk_heads = jnp.concatenate(blocks, axis=0)
-        gathered = lax.all_gather(chunk_heads, "seq", axis=1, tiled=True)
+        gathered = gather_around(chunk_heads, "seq", 1)
         projected = jnp.dot(gathered, out_weight, preferred_element_type=jnp.float32)
         pieces.append(lax.psum_scatter(projected, "tensor", scatter_dimension=0, tiled=True))
     summed = jnp.concatenate(pieces, axis=0)

time: 440 us -> 424 us (0.964)
  waiting for transfers between devices: 299 us -> 105 us
  local copies, waits for them, and re-layouts: 15.3 us -> 133 us
  starting transfers between devices: 11.8 us -> 72.7 us
  matrix products: 62.2 us -> 57 us
    all_gather x4 -> x0, waiting for transfers between devices: 135 us -> none  [on_device(): gathered = lax.all_gather(chunk_heads, 'seq', axis=1, tiled=True)]
    reduce_scatter x4, waiting for transfers between devices: 130 us -> 32.2 us  [on_device(): lax.psum_scatter(projected, 'tensor', scatter_dimension=0, tiled=True)]
    unnamed x19 -> x193, local copies, waits for them, and re-layouts: 9.34 us -> 74.7 us
    ppermute x0 -> x60, starting transfers between devices: none -> 62.2 us  [the longest x28 42.7 us: gather_around(): upper.append(lax.ppermute(upper[-1] if upper else x, axis, back))]
    ppermute x0 -> x60, waiting for transfers between devices: none -> 40.9 us  [the longest x32 28.1 us: gather_around(): lower.append(lax.ppermute(lower[-1] if lower else x, axis, pairs))]
    transpose x0 -> x4, local copies, waits for them, and re-layouts: none -> 25.6 us  [in_order(): tiles = jnp.moveaxis(tiles, 0, dim)]
    gather x0 -> x4, local copies, waits for them, and re-layouts: none -> 21.8 us  [gather_around(): parts = parts[(jnp.arange(count) - shift) % count]]
    dot_general x16, matrix products: 17.8 us -> 12.8 us  [attend_rows(): jnp.einsum('qd,kd->qk', query_block, key_head[:key_end], preferred_elemen...]
  transfers between devices with their start and end apart: 10 -> 66, of which waited for: 9 -> 20; matrix products, arithmetic and copies ran while one was open for 21% -> 49% of each run, Pallas kernels for 0% -> 0%
where the time goes in v1:
time: 424 us; the launch traced here: 419 us
  local copies, waits for them, and re-layouts  133 us (31%)
  waiting for transfers between devices  105 us (25%)
  starting transfers between devices  72.7 us (17%)
  matrix products  57 us (13%)
  other arithmetic  35.9 us (8%)
  between operations  14.4 us (3%)
    unnamed x193, local copies, waits for them, and re-layouts  74.7 us
    ppermute x28, starting transfers between devices, gather_around(): upper.append(lax.ppermute(upper[-1] if upper else x, axis, back))  42.7 us
    reduce_scatter x4, waiting for transfers between devices, on_device(): lax.psum_scatter(projected, 'tensor', scatter_dimension=0, tiled=True)  32.2 us
    all_to_all x1, waiting for transfers between devices, on_device(): lax.all_to_all(query_slab, 'seq', split_axis=2, concat_axis=0, tiled=True)  32.1 us
    ppermute x32, waiting for transfers between devices, gather_around(): lower.append(lax.ppermute(lower[-1] if lower else x, axis, pairs))  28.1 us
    transpose x4, local copies, waits for them, and re-layouts, in_order(): tiles = jnp.moveaxis(tiles, 0, dim)  25.6 us
    dot_general x4, matrix products, on_device(): jnp.dot(gathered, out_weight, preferred_element_type=jnp.float32)  23.7 us
    gather x4, local copies, waits for them, and re-layouts, gather_around(): parts = parts[(jnp.arange(count) - shift) % count]  21.8 us
  transfers between devices with their start and end apart: 66, of which 20 were waited for; matrix products, arithmetic and copies ran while one was open for 49% of the time, Pallas kernels for 0%

profile of v1, /device:TPU:1, one launch (start us, length us, event | category | flops | bytes accessed | tf_op | source)
XLA Modules:
  0.0 418.8 jit_solution(1755210666393819706)
XLA Ops:
  6.5 1.8 copy.55
  8.4 6.0 %copy.56 = bf16[256,1,2048]{0,1,2:T(2,128)(2,1)} copy(bf16[256,1,2048]{2,0,1:T(8,128)(2,1)} %bitcast.462) | data formatting | bytes 2097152 | tf_op jit(solution)/shard_map/reshape | solution.py:65
  14.9 11.6 %reduce = bf16[2048,256]{1,0:T(8,128)(2,1)S(1)} reduce(bf16[2048,1,256]{2,1,0:T(2,128)(2,1)} %bitcast.452, bf16[]{:T(256)} %broadcast.250), dimensions={1}, to_apply=%bitcast.366.reduce_sub_computation | reduce | bytes 2097154
  27.6 10.0 %all-to-all-start = ((bf16[16,2,16384]{2,1,0:T(2,128)(2,1)}), bf16[16,2,16384]{2,1,0:T(2,128)(2,1)S(1)}, u32[]{:S(2)}, u32[]{:S(2)}) async-start(bf16[16,2,16384]{2,1,0:T(2,128)(2,1)} %reshape.288), calls=%async_computation | async-start | bytes 2097152 | tf_op jit(solution)/shard_map/all_to_all | solution.py:66
  40.5 32.1 %all-to-all-done = bf16[16,2,16384]{2,1,0:T(2,128)(2,1)S(1)} async-done(((bf16[16,2,16384]{2,1,0:T(2,128)(2,1)}), bf16[16,2,16384]{2,1,0:T(2,128)(2,1)S(1)}, u32[]{:S(2)}, u32[]{:S(2)}) %all-to-all-start) | async-done | bytes 1048608 | tf_op jit(solution)/shard_map/all_to_all | solution.py:66
  72.5 3.5 reshape.289
  76.0 1.8 copy.77
  77.8 3.2 fusion.132
  81.0 1.9 fusion.30
  87.6 2.3 fusion.65
  89.9 1.7 fusion.69
  95.0 2.1 fusion.32
  101.3 2.2 fusion.64
  106.7 1.8 collective-permute-start.30
  110.3 1.7 fusion.33
  115.9 2.0 fusion.63
  124.4 1.9 fusion.70
  127.1 2.6 collective-permute-done.46
  129.7 2.5 collective-permute-start.47
  133.5 2.8 collective-permute-done.47
  137.9 1.9 fusion.66
  139.9 3.4 collective-permute-done.48
  144.4 5.9 %collective-permute-done.49 = bf16[1024,128]{1,0:T(8,128)(2,1)S(1)} collective-permute-done((bf16[1024,128]{1,0:T(8,128)(2,1)S(1)}, bf16[1024,128]{1,0:T(8,128)(2,1)S(1)}, u32[]{:S(2)}, u32[]{:S(2)}) %collective-permute-start.49) | collective-permute-done | bytes 262176 | tf_op jit(solution)/shard_map/ppermute | solution.py:27
  150.8 6.5 %collective-permute-done.50 = bf16[1024,128]{1,0:T(8,128)(2,1)S(1)} collective-permute-done((bf16[1024,128]{1,0:T(8,128)(2,1)S(1)}, bf16[1024,128]{1,0:T(8,128)(2,1)S(1)}, u32[]{:S(2)}, u32[]{:S(2)}) %collective-permute-start.50) | collective-permute-done | bytes 262176 | tf_op jit(solution)/shard_map/ppermute | solution.py:27
  158.0 6.3 %collective-permute-done.51 = bf16[1024,128]{1,0:T(8,128)(2,1)S(1)} collective-permute-done((bf16[1024,128]{1,0:T(8,128)(2,1)S(1)}, bf16[1024,128]{1,0:T(8,128)(2,1)S(1)}, u32[]{:S(2)}, u32[]{:S(2)}) %collective-permute-start.51) | collective-permute-done | bytes 262176 | tf_op jit(solution)/shard_map/ppermute | solution.py:27
  164.7 6.0 %collective-permute-start.23 = (bf16[1024,128]{1,0:T(8,128)(2,1)S(1)}, bf16[1024,128]{1,0:T(8,128)(2,1)S(1)}, u32[]{:S(2)}, u32[]{:S(2)}) collective-permute-start(bf16[1024,128]{1,0:T(8,128)(2,1)S(1)} %pad_maximum_fusion.1), channel_id=1, source_target_pairs={{4,0},{8,4},{12,8},{16,12},{20,16},{24,20},{28,24},{32,28},{36,32}... | collective-permute-start | bytes 786440 | tf_op jit(solution)/shard_map/ppermute | solution.py:29
  171.3 6.0 %collective-permute-start.8 = (bf16[1024,128]{1,0:T(8,128)(2,1)S(1)}, bf16[1024,128]{1,0:T(8,128)(2,1)S(1)}, u32[]{:S(2)}, u32[]{:S(2)}) collective-permute-start(bf16[1024,128]{1,0:T(8,128)(2,1)S(1)} %pad_maximum_fusion), channel_id=1, source_target_pairs={{4,0},{8,4},{12,8},{16,12},{20,16},{24,20},{28,24},{32,28},{36,32}... | collective-permute-start | bytes 786440 | tf_op jit(solution)/shard_map/ppermute | solution.py:29
  178.8 1.7 collective-permute-start.31
  180.5 1.7 collective-permute-start.16
  192.0 1.7 collective-permute-start.17
  204.2 2.0 collective-permute-start.26
  207.3 1.9 collective-permute-start.57
  212.8 1.9 collective-permute-start.42
  215.8 1.8 collective-permute-start.58
  221.3 2.6 collective-permute-done.58
  225.8 3.1 collective-permute-start.12
  229.0 1.7 collective-permute-start.20
  232.2 5.4 %gather_fusion.3 = bf16[16,1024,128]{2,1,0:T(8,128)(2,1)} fusion(bf16[16,1024,128]{2,1,0:T(8,128)(2,1)} %bitcast_dynamic-update-slice_fusion, s32[1024]{0:T(1024)} %pad_clamp_fusion), kind=kCustom, calls=%fused_computation.3 | custom fusion | bytes 8388672 | tf_op jit(solution)/shard_map/gather | solution.py:32
  237.7 6.4 %copy.76 = bf16[1024,16,128]{0,2,1:T(8,128)(2,1)} copy(bf16[1024,16,128]{2,0,1:T(8,128)(2,1)} %bitcast.445) | data formatting | bytes 8388608 | tf_op jit(solution)/shard_map/transpose | solution.py:15
  244.1 2.6 collective-permute-start.28
  246.7 2.9 collective-permute-start.13
  249.7 5.9 %fusion.151 = f32[1024,512]{1,0:T(8,128)} fusion(bf16[1024,2048]{0,1:T(8,128)(2,1)} %bitcast.443, bf16[2048,512]{1,0:T(8,128)(2,1)S(1)} %copy-done), kind=kOutput, calls=%fused_computation.364 | convolution fusion | flops 2147483648 | bytes 8388608 | tf_op jit(solution)/shard_map/dot_general | solution.py:93
  256.2 2.9 collective-permute-start.29
  263.0 1.7 bitcast_dynamic-update-slice_fusion.30
  266.4 1.7 bitcast_dynamic-update-slice_fusion.28
  269.8 1.7 bitcast_dynamic-update-slice_fusion.26
  281.6 5.4 %gather_fusion.2 = bf16[16,1024,128]{2,1,0:T(8,128)(2,1)} fusion(bf16[16,1024,128]{2,1,0:T(8,128)(2,1)} %bitcast_dynamic-update-slice_fusion.16, s32[1024]{0:T(1024)} %pad_clamp_fusion), kind=kCustom, calls=%fused_computation.2 | custom fusion | bytes 8388672 | tf_op jit(solution)/shard_map/gather | solution.py:32
  287.0 6.4 %copy.71 = bf16[1024,16,128]{0,2,1:T(8,128)(2,1)} copy(bf16[1024,16,128]{2,0,1:T(8,128)(2,1)} %bitcast.446) | data formatting | bytes 8388608 | tf_op jit(solution)/shard_map/transpose | solution.py:15
  293.4 6.0 %fusion.150 = f32[1024,512]{1,0:T(8,128)} fusion(bf16[1024,2048]{0,1:T(8,128)(2,1)} %bitcast.447, bf16[2048,512]{1,0:T(8,128)(2,1)S(1)} %copy-done), kind=kOutput, calls=%fused_computation.363 | convolution fusion | flops 2147483648 | bytes 8388608 | tf_op jit(solution)/shard_map/dot_general | solution.py:93
  299.7 1.7 bitcast_dynamic-update-slice_fusion.47
  301.5 1.7 bitcast_dynamic-update-slice_fusion.46
  308.2 1.7 bitcast_dynamic-update-slice_fusion.42
  309.9 1.7 bitcast_dynamic-update-slice_fusion.41
  320.9 5.5 %gather_fusion.1 = bf16[16,1024,128]{2,1,0:T(8,128)(2,1)} fusion(bf16[16,1024,128]{2,1,0:T(8,128)(2,1)} %bitcast_dynamic-update-slice_fusion.32, s32[1024]{0:T(1024)} %pad_clamp_fusion), kind=kCustom, calls=%fused_computation.1 | custom fusion | bytes 8388672 | tf_op jit(solution)/shard_map/gather | solution.py:32
  326.4 6.4 %copy.66 = bf16[1024,16,128]{0,2,1:T(8,128)(2,1)} copy(bf16[1024,16,128]{2,0,1:T(8,128)(2,1)} %bitcast.448) | data formatting | bytes 8388608 | tf_op jit(solution)/shard_map/transpose | solution.py:15
  332.8 5.9 %fusion.149 = f32[1024,512]{1,0:T(8,128)} fusion(bf16[1024,2048]{0,1:T(8,128)(2,1)} %bitcast.449, bf16[2048,512]{1,0:T(8,128)(2,1)S(1)} %copy-done), kind=kOutput, calls=%fused_computation.362 | convolution fusion | flops 2147483648 | bytes 8388608 | tf_op jit(solution)/shard_map/dot_general | solution.py:93
  338.8 1.8 bitcast_dynamic-update-slice_fusion.63
  340.5 1.7 bitcast_dynamic-update-slice_fusion.62
  347.2 1.7 bitcast_dynamic-update-slice_fusion.58
  359.0 5.5 %gather_fusion = bf16[16,1024,128]{2,1,0:T(8,128)(2,1)} fusion(bf16[16,1024,128]{2,1,0:T(8,128)(2,1)} %bitcast_dynamic-update-slice_fusion.48, s32[1024]{0:T(1024)} %pad_clamp_fusion), kind=kCustom, calls=%fused_computation | custom fusion | bytes 8388672 | tf_op jit(solution)/shard_map/gather | solution.py:32
  364.5 6.4 %copy.61 = bf16[1024,16,128]{0,2,1:T(8,128)(2,1)} copy(bf16[1024,16,128]{2,0,1:T(8,128)(2,1)} %bitcast.444) | data formatting | bytes 8388608 | tf_op jit(solution)/shard_map/transpose | solution.py:15
  370.9 6.0 %fusion.148 = f32[1024,512]{1,0:T(8,128)} fusion(bf16[1024,2048]{0,1:T(8,128)(2,1)} %bitcast.450, bf16[2048,512]{1,0:T(8,128)(2,1)S(1)} %copy-done), kind=kOutput, calls=%fused_computation.361 | convolution fusion | flops 2147483648 | bytes 8388608 | tf_op jit(solution)/shard_map/dot_general | solution.py:93
  377.0 32.2 %reduce-scatter.5.cloned.1.call-done = f32[256,512]{1,0:T(8,128)} async-done(((f32[1024,512]{1,0:T(8,128)}), f32[256,512]{1,0:T(8,128)}) %reduce-scatter.5.cloned.1.call-update) | async-done | bytes 524304 | tf_op jit(solution)/shard_map/reduce_scatter | solution.py:94
  409.2 2.8 fusion.36
  (369 shorter events, 121.2 us)
Async XLA Ops:
  6.5 71.3 %all-gather.2.cloned.1.call-start = ((), (), s32[]{:S(2)}) async-start(), calls=%async_computation.5 | async-start | bytes 4456448 | tf_op jit(solution)/shard_map/all_gather | solution.py:70
  27.6 44.9 %all-to-all-start = ((bf16[16,2,16384]{2,1,0:T(2,128)(2,1)}), bf16[16,2,16384]{2,1,0:T(2,128)(2,1)S(1)}, u32[]{:S(2)}, u32[]{:S(2)}) async-start(bf16[16,2,16384]{2,1,0:T(2,128)(2,1)} %reshape.288), calls=%async_computation | async-start | bytes 2097152 | tf_op jit(solution)/shard_map/all_to_all | solution.py:66
  37.6 339.3 %reduce-scatter.11.cloned.1.call-start = ((), (), s32[]{:S(2)}) async-start(), calls=%async_computation.9 | async-start | bytes 2621440 | tf_op jit(solution)/shard_map/reduce_scatter | solution.py:94
  93.4 32.9 %collective-permute-start.45 = (bf16[1024,128]{1,0:T(8,128)(2,1)S(1)}, bf16[1024,128]{1,0:T(8,128)(2,1)S(1)}, u32[]{:S(2)}, u32[]{:S(2)}) collective-permute-start(bf16[1024,128]{1,0:T(8,128)(2,1)S(1)} %pad_maximum_fusion.3), channel_id=1, source_target_pairs={{0,4},{4,8},{8,12},{12,16},{16,20},{20,24},{24,28},{28,32},{32,36}... | collective-permute-start | bytes 786440 | tf_op jit(solution)/shard_map/ppermute | solution.py:27
  93.9 70.8 %collective-permute-start.53 = (bf16[1024,128]{1,0:T(8,128)(2,1)S(1)}, bf16[1024,128]{1,0:T(8,128)(2,1)S(1)}, u32[]{:S(2)}, u32[]{:S(2)}) collective-permute-start(bf16[1024,128]{1,0:T(8,128)(2,1)S(1)} %pad_maximum_fusion.3), channel_id=1, source_target_pairs={{4,0},{8,4},{12,8},{16,12},{20,16},{24,20},{28,24},{32,28},{36,32}... | collective-permute-start | bytes 786440 | tf_op jit(solution)/shard_map/ppermute | solution.py:29
  106.7 64.0 %collective-permute-start.30 = (bf16[1024,128]{1,0:T(8,128)(2,1)S(1)}, bf16[1024,128]{1,0:T(8,128)(2,1)S(1)}, u32[]{:S(2)}, u32[]{:S(2)}) collective-permute-start(bf16[1024,128]{1,0:T(8,128)(2,1)S(1)} %pad_maximum_fusion.2), channel_id=1, source_target_pairs={{0,4},{4,8},{8,12},{12,16},{16,20},{20,24},{24,28},{28,32},{32,36}... | collective-permute-start | bytes 786440 | tf_op jit(solution)/shard_map/ppermute | solution.py:27
  108.4 70.3 %collective-permute-start.38 = (bf16[1024,128]{1,0:T(8,128)(2,1)S(1)}, bf16[1024,128]{1,0:T(8,128)(2,1)S(1)}, u32[]{:S(2)}, u32[]{:S(2)}) collective-permute-start(bf16[1024,128]{1,0:T(8,128)(2,1)S(1)} %pad_maximum_fusion.2), channel_id=1, source_target_pairs={{4,0},{8,4},{12,8},{16,12},{20,16},{24,20},{28,24},{32,28},{36,32}... | collective-permute-start | bytes 786440 | tf_op jit(solution)/shard_map/ppermute | solution.py:29
  120.8 58.0 %collective-permute-start.15 = (bf16[1024,128]{1,0:T(8,128)(2,1)S(1)}, bf16[1024,128]{1,0:T(8,128)(2,1)S(1)}, u32[]{:S(2)}, u32[]{:S(2)}) collective-permute-start(bf16[1024,128]{1,0:T(8,128)(2,1)S(1)} %pad_maximum_fusion.1), channel_id=1, source_target_pairs={{0,4},{4,8},{8,12},{12,16},{16,20},{20,24},{24,28},{28,32},{32,36}... | collective-permute-start | bytes 786440 | tf_op jit(solution)/shard_map/ppermute | solution.py:27
  129.7 6.6 %collective-permute-start.47 = (bf16[1024,128]{1,0:T(8,128)(2,1)S(1)}, bf16[1024,128]{1,0:T(8,128)(2,1)S(1)}, u32[]{:S(2)}, u32[]{:S(2)}) collective-permute-start(bf16[1024,128]{1,0:T(8,128)(2,1)S(1)} %collective-permute-done.46), channel_id=1, source_target_pairs={{0,4},{4,8},{8,12},{12,16},{16,20},{20,24},{24,28},{28,32},{32,36}... | collective-permute-start | bytes 786440 | tf_op jit(solution)/shard_map/ppermute | solution.py:27
  136.3 7.0 %collective-permute-start.48 = (bf16[1024,128]{1,0:T(8,128)(2,1)S(1)}, bf16[1024,128]{1,0:T(8,128)(2,1)S(1)}, u32[]{:S(2)}, u32[]{:S(2)}) collective-permute-start(bf16[1024,128]{1,0:T(8,128)(2,1)S(1)} %collective-permute-done.47), channel_id=1, source_target_pairs={{0,4},{4,8},{8,12},{12,16},{16,20},{20,24},{24,28},{28,32},{32,36}... | collective-permute-start | bytes 786440 | tf_op jit(solution)/shard_map/ppermute | solution.py:27
  143.3 7.0 %collective-permute-start.49 = (bf16[1024,128]{1,0:T(8,128)(2,1)S(1)}, bf16[1024,128]{1,0:T(8,128)(2,1)S(1)}, u32[]{:S(2)}, u32[]{:S(2)}) collective-permute-start(bf16[1024,128]{1,0:T(8,128)(2,1)S(1)} %collective-permute-done.48), channel_id=1, source_target_pairs={{0,4},{4,8},{8,12},{12,16},{16,20},{20,24},{24,28},{28,32},{32,36}... | collective-permute-start | bytes 786440 | tf_op jit(solution)/shard_map/ppermute | solution.py:27
  150.3 7.0 %collective-permute-start.50 = (bf16[1024,128]{1,0:T(8,128)(2,1)S(1)}, bf16[1024,128]{1,0:T(8,128)(2,1)S(1)}, u32[]{:S(2)}, u32[]{:S(2)}) collective-permute-start(bf16[1024,128]{1,0:T(8,128)(2,1)S(1)} %collective-permute-done.49), channel_id=1, source_target_pairs={{0,4},{4,8},{8,12},{12,16},{16,20},{20,24},{24,28},{28,32},{32,36}... | collective-permute-start | bytes 786440 | tf_op jit(solution)/shard_map/ppermute | solution.py:27
  157.3 7.0 %collective-permute-start.51 = (bf16[1024,128]{1,0:T(8,128)(2,1)S(1)}, bf16[1024,128]{1,0:T(8,128)(2,1)S(1)}, u32[]{:S(2)}, u32[]{:S(2)}) collective-permute-start(bf16[1024,128]{1,0:T(8,128)(2,1)S(1)} %collective-permute-done.50), channel_id=1, source_target_pairs={{0,4},{4,8},{8,12},{12,16},{16,20},{20,24},{24,28},{28,32},{32,36}... | collective-permute-start | bytes 786440 | tf_op jit(solution)/shard_map/ppermute | solution.py:27
  164.3 7.0 %collective-permute-start.52 = (bf16[1024,128]{1,0:T(8,128)(2,1)S(1)}, bf16[1024,128]{1,0:T(8,128)(2,1)S(1)}, u32[]{:S(2)}, u32[]{:S(2)}) collective-permute-start(bf16[1024,128]{1,0:T(8,128)(2,1)S(1)} %collective-permute-done.51), channel_id=1, source_target_pairs={{0,4},{4,8},{8,12},{12,16},{16,20},{20,24},{24,28},{28,32},{32,36}... | collective-permute-start | bytes 786440 | tf_op jit(solution)/shard_map/ppermute | solution.py:27
  164.7 15.8 %collective-permute-start.23 = (bf16[1024,128]{1,0:T(8,128)(2,1)S(1)}, bf16[1024,128]{1,0:T(8,128)(2,1)S(1)}, u32[]{:S(2)}, u32[]{:S(2)}) collective-permute-start(bf16[1024,128]{1,0:T(8,128)(2,1)S(1)} %pad_maximum_fusion.1), channel_id=1, source_target_pairs={{4,0},{8,4},{12,8},{16,12},{20,16},{24,20},{28,24},{32,28},{36,32}... | collective-permute-start | bytes 786440 | tf_op jit(solution)/shard_map/ppermute | solution.py:29
  170.7 9.8 %collective-permute-start = (bf16[1024,128]{1,0:T(8,128)(2,1)S(1)}, bf16[1024,128]{1,0:T(8,128)(2,1)S(1)}, u32[]{:S(2)}, u32[]{:S(2)}) collective-permute-start(bf16[1024,128]{1,0:T(8,128)(2,1)S(1)} %pad_maximum_fusion), channel_id=1, source_target_pairs={{0,4},{4,8},{8,12},{12,16},{16,20},{20,24},{24,28},{28,32},{32,36}... | collective-permute-start | bytes 786440 | tf_op jit(solution)/shard_map/ppermute | solution.py:27
  171.3 11.0 %collective-permute-start.8 = (bf16[1024,128]{1,0:T(8,128)(2,1)S(1)}, bf16[1024,128]{1,0:T(8,128)(2,1)S(1)}, u32[]{:S(2)}, u32[]{:S(2)}) collective-permute-start(bf16[1024,128]{1,0:T(8,128)(2,1)S(1)} %pad_maximum_fusion), channel_id=1, source_target_pairs={{4,0},{8,4},{12,8},{16,12},{20,16},{24,20},{28,24},{32,28},{36,32}... | collective-permute-start | bytes 786440 | tf_op jit(solution)/shard_map/ppermute | solution.py:29
  178.8 6.7 %collective-permute-start.31 = (bf16[1024,128]{1,0:T(8,128)(2,1)S(1)}, bf16[1024,128]{1,0:T(8,128)(2,1)S(1)}, u32[]{:S(2)}, u32[]{:S(2)}) collective-permute-start(bf16[1024,128]{1,0:T(8,128)(2,1)S(1)} %collective-permute-done.30), channel_id=1, source_target_pairs={{0,4},{4,8},{8,12},{12,16},{16,20},{20,24},{24,28},{28,32},{32,36}... | collective-permute-start | bytes 786440 | tf_op jit(solution)/shard_map/ppermute | solution.py:27
  180.5 7.1 %collective-permute-start.39 = (bf16[1024,128]{1,0:T(8,128)(2,1)S(1)}, bf16[1024,128]{1,0:T(8,128)(2,1)S(1)}, u32[]{:S(2)}, u32[]{:S(2)}) collective-permute-start(bf16[1024,128]{1,0:T(8,128)(2,1)S(1)} %collective-permute-done.38), channel_id=1, source_target_pairs={{4,0},{8,4},{12,8},{16,12},{20,16},{24,20},{28,24},{32,28},{36,32}... | collective-permute-start | bytes 786440 | tf_op jit(solution)/shard_map/ppermute | solution.py:29
  180.5 8.6 %collective-permute-start.16 = (bf16[1024,128]{1,0:T(8,128)(2,1)S(1)}, bf16[1024,128]{1,0:T(8,128)(2,1)S(1)}, u32[]{:S(2)}, u32[]{:S(2)}) collective-permute-start(bf16[1024,128]{1,0:T(8,128)(2,1)S(1)} %collective-permute-done.15), channel_id=1, source_target_pairs={{0,4},{4,8},{8,12},{12,16},{16,20},{20,24},{24,28},{28,32},{32,36}... | collective-permute-start | bytes 786440 | tf_op jit(solution)/shard_map/ppermute | solution.py:27
  182.3 8.2 %collective-permute-start.24 = (bf16[1024,128]{1,0:T(8,128)(2,1)S(1)}, bf16[1024,128]{1,0:T(8,128)(2,1)S(1)}, u32[]{:S(2)}, u32[]{:S(2)}) collective-permute-start(bf16[1024,128]{1,0:T(8,128)(2,1)S(1)} %collective-permute-done.23), channel_id=1, source_target_pairs={{4,0},{8,4},{12,8},{16,12},{20,16},{24,20},{28,24},{32,28},{36,32}... | collective-permute-start | bytes 786440 | tf_op jit(solution)/shard_map/ppermute | solution.py:29
  184.9 7.1 %collective-permute-start.1 = (bf16[1024,128]{1,0:T(8,128)(2,1)S(1)}, bf16[1024,128]{1,0:T(8,128)(2,1)S(1)}, u32[]{:S(2)}, u32[]{:S(2)}) collective-permute-start(bf16[1024,128]{1,0:T(8,128)(2,1)S(1)} %collective-permute-done), channel_id=1, source_target_pairs={{0,4},{4,8},{8,12},{12,16},{16,20},{20,24},{24,28},{28,32},{32,36}... | collective-permute-start | bytes 786440 | tf_op jit(solution)/shard_map/ppermute | solution.py:27
  185.5 8.2 %collective-permute-start.9 = (bf16[1024,128]{1,0:T(8,128)(2,1)S(1)}, bf16[1024,128]{1,0:T(8,128)(2,1)S(1)}, u32[]{:S(2)}, u32[]{:S(2)}) collective-permute-start(bf16[1024,128]{1,0:T(8,128)(2,1)S(1)} %collective-permute-done.8), channel_id=1, source_target_pairs={{4,0},{8,4},{12,8},{16,12},{20,16},{24,20},{28,24},{32,28},{36,32}... | collective-permute-start | bytes 786440 | tf_op jit(solution)/shard_map/ppermute | solution.py:29
  187.7 8.4 %collective-permute-start.55 = (bf16[1024,128]{1,0:T(8,128)(2,1)S(1)}, bf16[1024,128]{1,0:T(8,128)(2,1)S(1)}, u32[]{:S(2)}, u32[]{:S(2)}) collective-permute-start(bf16[1024,128]{1,0:T(8,128)(2,1)S(1)} %collective-permute-done.54), channel_id=1, source_target_pairs={{4,0},{8,4},{12,8},{16,12},{20,16},{24,20},{28,24},{32,28},{36,32}... | collective-permute-start | bytes 786440 | tf_op jit(solution)/shard_map/ppermute | solution.py:29
  189.2 6.9 %collective-permute-start.32 = (bf16[1024,128]{1,0:T(8,128)(2,1)S(1)}, bf16[1024,128]{1,0:T(8,128)(2,1)S(1)}, u32[]{:S(2)}, u32[]{:S(2)}) collective-permute-start(bf16[1024,128]{1,0:T(8,128)(2,1)S(1)} %collective-permute-done.31), channel_id=1, source_target_pairs={{0,4},{4,8},{8,12},{12,16},{16,20},{20,24},{24,28},{28,32},{32,36}... | collective-permute-start | bytes 786440 | tf_op jit(solution)/shard_map/ppermute | solution.py:27
  190.5 8.4 %collective-permute-start.40 = (bf16[1024,128]{1,0:T(8,128)(2,1)S(1)}, bf16[1024,128]{1,0:T(8,128)(2,1)S(1)}, u32[]{:S(2)}, u32[]{:S(2)}) collective-permute-start(bf16[1024,128]{1,0:T(8,128)(2,1)S(1)} %collective-permute-done.39), channel_id=1, source_target_pairs={{4,0},{8,4},{12,8},{16,12},{20,16},{24,20},{28,24},{32,28},{36,32}... | collective-permute-start | bytes 786440 | tf_op jit(solution)/shard_map/ppermute | solution.py:29
  192.0 9.8 %collective-permute-start.17 = (bf16[1024,128]{1,0:T(8,128)(2,1)S(1)}, bf16[1024,128]{1,0:T(8,128)(2,1)S(1)}, u32[]{:S(2)}, u32[]{:S(2)}) collective-permute-start(bf16[1024,128]{1,0:T(8,128)(2,1)S(1)} %collective-permute-done.16), channel_id=1, source_target_pairs={{0,4},{4,8},{8,12},{12,16},{16,20},{20,24},{24,28},{28,32},{32,36}... | collective-permute-start | bytes 786440 | tf_op jit(solution)/shard_map/ppermute | solution.py:27
  193.7 8.4 %collective-permute-start.25 = (bf16[1024,128]{1,0:T(8,128)(2,1)S(1)}, bf16[1024,128]{1,0:T(8,128)(2,1)S(1)}, u32[]{:S(2)}, u32[]{:S(2)}) collective-permute-start(bf16[1024,128]{1,0:T(8,128)(2,1)S(1)} %collective-permute-done.24), channel_id=1, source_target_pairs={{4,0},{8,4},{12,8},{16,12},{20,16},{24,20},{28,24},{32,28},{36,32}... | collective-permute-start | bytes 786440 | tf_op jit(solution)/shard_map/ppermute | solution.py:29
  196.1 7.2 %collective-permute-start.2 = (bf16[1024,128]{1,0:T(8,128)(2,1)S(1)}, bf16[1024,128]{1,0:T(8,128)(2,1)S(1)}, u32[]{:S(2)}, u32[]{:S(2)}) collective-permute-start(bf16[1024,128]{1,0:T(8,128)(2,1)S(1)} %collective-permute-done.1), channel_id=1, source_target_pairs={{0,4},{4,8},{8,12},{12,16},{16,20},{20,24},{24,28},{28,32},{32,36}... | collective-permute-start | bytes 786440 | tf_op jit(solution)/shard_map/ppermute | solution.py:27
  196.1 8.1 %collective-permute-start.10 = (bf16[1024,128]{1,0:T(8,128)(2,1)S(1)}, bf16[1024,128]{1,0:T(8,128)(2,1)S(1)}, u32[]{:S(2)}, u32[]{:S(2)}) collective-permute-start(bf16[1024,128]{1,0:T(8,128)(2,1)S(1)} %collective-permute-done.9), channel_id=1, source_target_pairs={{4,0},{8,4},{12,8},{16,12},{20,16},{24,20},{28,24},{32,28},{36,32}... | collective-permute-start | bytes 786440 | tf_op jit(solution)/shard_map/ppermute | solution.py:29
  198.9 8.4 %collective-permute-start.56 = (bf16[1024,128]{1,0:T(8,128)(2,1)S(1)}, bf16[1024,128]{1,0:T(8,128)(2,1)S(1)}, u32[]{:S(2)}, u32[]{:S(2)}) collective-permute-start(bf16[1024,128]{1,0:T(8,128)(2,1)S(1)} %collective-permute-done.55), channel_id=1, source_target_pairs={{4,0},{8,4},{12,8},{16,12},{20,16},{24,20},{28,24},{32,28},{36,32}... | collective-permute-start | bytes 786440 | tf_op jit(solution)/shard_map/ppermute | solution.py:29
  201.8 8.9 %collective-permute-start.33 = (bf16[1024,128]{1,0:T(8,128)(2,1)S(1)}, bf16[1024,128]{1,0:T(8,128)(2,1)S(1)}, u32[]{:S(2)}, u32[]{:S(2)}) collective-permute-start(bf16[1024,128]{1,0:T(8,128)(2,1)S(1)} %collective-permute-done.32), channel_id=1, source_target_pairs={{0,4},{4,8},{8,12},{12,16},{16,20},{20,24},{24,28},{28,32},{32,36}... | collective-permute-start | bytes 786440 | tf_op jit(solution)/shard_map/ppermute | solution.py:27
  202.1 8.6 %collective-permute-start.41 = (bf16[1024,128]{1,0:T(8,128)(2,1)S(1)}, bf16[1024,128]{1,0:T(8,128)(2,1)S(1)}, u32[]{:S(2)}, u32[]{:S(2)}) collective-permute-start(bf16[1024,128]{1,0:T(8,128)(2,1)S(1)} %collective-permute-done.40), channel_id=1, source_target_pairs={{4,0},{8,4},{12,8},{16,12},{20,16},{24,20},{28,24},{32,28},{36,32}... | collective-permute-start | bytes 786440 | tf_op jit(solution)/shard_map/ppermute | solution.py:29
  203.3 8.4 %collective-permute-start.18 = (bf16[1024,128]{1,0:T(8,128)(2,1)S(1)}, bf16[1024,128]{1,0:T(8,128)(2,1)S(1)}, u32[]{:S(2)}, u32[]{:S(2)}) collective-permute-start(bf16[1024,128]{1,0:T(8,128)(2,1)S(1)} %collective-permute-done.17), channel_id=1, source_target_pairs={{0,4},{4,8},{8,12},{12,16},{16,20},{20,24},{24,28},{28,32},{32,36}... | collective-permute-start | bytes 786440 | tf_op jit(solution)/shard_map/ppermute | solution.py:27
  204.2 8.6 %collective-permute-start.26 = (bf16[1024,128]{1,0:T(8,128)(2,1)S(1)}, bf16[1024,128]{1,0:T(8,128)(2,1)S(1)}, u32[]{:S(2)}, u32[]{:S(2)}) collective-permute-start(bf16[1024,128]{1,0:T(8,128)(2,1)S(1)} %collective-permute-done.25), channel_id=1, source_target_pairs={{4,0},{8,4},{12,8},{16,12},{20,16},{24,20},{28,24},{32,28},{36,32}... | collective-permute-start | bytes 786440 | tf_op jit(solution)/shard_map/ppermute | solution.py:29
  207.3 8.4 %collective-permute-start.57 = (bf16[1024,128]{1,0:T(8,128)(2,1)S(1)}, bf16[1024,128]{1,0:T(8,128)(2,1)S(1)}, u32[]{:S(2)}, u32[]{:S(2)}) collective-permute-start(bf16[1024,128]{1,0:T(8,128)(2,1)S(1)} %collective-permute-done.56), channel_id=1, source_target_pairs={{4,0},{8,4},{12,8},{16,12},{20,16},{24,20},{28,24},{32,28},{36,32}... | collective-permute-start | bytes 786440 | tf_op jit(solution)/shard_map/ppermute | solution.py:29
  210.7 8.4 %collective-permute-start.3 = (bf16[1024,128]{1,0:T(8,128)(2,1)S(1)}, bf16[1024,128]{1,0:T(8,128)(2,1)S(1)}, u32[]{:S(2)}, u32[]{:S(2)}) collective-permute-start(bf16[1024,128]{1,0:T(8,128)(2,1)S(1)} %collective-permute-done.2), channel_id=1, source_target_pairs={{0,4},{4,8},{8,12},{12,16},{16,20},{20,24},{24,28},{28,32},{32,36}... | collective-permute-start | bytes 786440 | tf_op jit(solution)/shard_map/ppermute | solution.py:27
  210.7 8.3 %collective-permute-start.11 = (bf16[1024,128]{1,0:T(8,128)(2,1)S(1)}, bf16[1024,128]{1,0:T(8,128)(2,1)S(1)}, u32[]{:S(2)}, u32[]{:S(2)}) collective-permute-start(bf16[1024,128]{1,0:T(8,128)(2,1)S(1)} %collective-permute-done.10), channel_id=1, source_target_pairs={{4,0},{8,4},{12,8},{16,12},{20,16},{24,20},{28,24},{32,28},{36,32}... | collective-permute-start | bytes 786440 | tf_op jit(solution)/shard_map/ppermute | solution.py:29
  211.7 8.8 %collective-permute-start.34 = (bf16[1024,128]{1,0:T(8,128)(2,1)S(1)}, bf16[1024,128]{1,0:T(8,128)(2,1)S(1)}, u32[]{:S(2)}, u32[]{:S(2)}) collective-permute-start(bf16[1024,128]{1,0:T(8,128)(2,1)S(1)} %collective-permute-done.33), channel_id=1, source_target_pairs={{0,4},{4,8},{8,12},{12,16},{16,20},{20,24},{24,28},{28,32},{32,36}... | collective-permute-start | bytes 786440 | tf_op jit(solution)/shard_map/ppermute | solution.py:27
  212.8 8.4 %collective-permute-start.42 = (bf16[1024,128]{1,0:T(8,128)(2,1)S(1)}, bf16[1024,128]{1,0:T(8,128)(2,1)}, u32[]{:S(2)}, u32[]{:S(2)}) collective-permute-start(bf16[1024,128]{1,0:T(8,128)(2,1)S(1)} %collective-permute-done.41), channel_id=1, source_target_pairs={{4,0},{8,4},{12,8},{16,12},{20,16},{24,20},{28,24},{32,28},{36,32}... | collective-permute-start | bytes 786440 | tf_op jit(solution)/shard_map/ppermute | solution.py:29
  215.8 8.1 %collective-permute-start.58 = (bf16[1024,128]{1,0:T(8,128)(2,1)S(1)}, bf16[1024,128]{1,0:T(8,128)(2,1)S(1)}, u32[]{:S(2)}, u32[]{:S(2)}) collective-permute-start(bf16[1024,128]{1,0:T(8,128)(2,1)S(1)} %collective-permute-done.57), channel_id=1, source_target_pairs={{4,0},{8,4},{12,8},{16,12},{20,16},{24,20},{28,24},{32,28},{36,32}... | collective-permute-start | bytes 786440 | tf_op jit(solution)/shard_map/ppermute | solution.py:29
  219.0 6.7 %collective-permute-start.19 = (bf16[1024,128]{1,0:T(8,128)(2,1)S(1)}, bf16[1024,128]{1,0:T(8,128)(2,1)}, u32[]{:S(2)}, u32[]{:S(2)}) collective-permute-start(bf16[1024,128]{1,0:T(8,128)(2,1)S(1)} %collective-permute-done.18), channel_id=1, source_target_pairs={{0,4},{4,8},{8,12},{12,16},{16,20},{20,24},{24,28},{28,32},{32,36}... | collective-permute-start | bytes 786440 | tf_op jit(solution)/shard_map/ppermute | solution.py:27
  219.1 9.8 %collective-permute-start.27 = (bf16[1024,128]{1,0:T(8,128)(2,1)S(1)}, bf16[1024,128]{1,0:T(8,128)(2,1)}, u32[]{:S(2)}, u32[]{:S(2)}) collective-permute-start(bf16[1024,128]{1,0:T(8,128)(2,1)S(1)} %collective-permute-done.26), channel_id=1, source_target_pairs={{4,0},{8,4},{12,8},{16,12},{20,16},{24,20},{28,24},{32,28},{36,32}... | collective-permute-start | bytes 786440 | tf_op jit(solution)/shard_map/ppermute | solution.py:29
  220.5 8.5 %collective-permute-start.4 = (bf16[1024,128]{1,0:T(8,128)(2,1)S(1)}, bf16[1024,128]{1,0:T(8,128)(2,1)}, u32[]{:S(2)}, u32[]{:S(2)}) collective-permute-start(bf16[1024,128]{1,0:T(8,128)(2,1)S(1)} %collective-permute-done.3), channel_id=1, source_target_pairs={{0,4},{4,8},{8,12},{12,16},{16,20},{20,24},{24,28},{28,32},{32,36}... | collective-permute-start | bytes 786440 | tf_op jit(solution)/shard_map/ppermute | solution.py:27
  221.3 9.4 %collective-permute-start.35 = (bf16[1024,128]{1,0:T(8,128)(2,1)S(1)}, bf16[1024,128]{1,0:T(8,128)(2,1)}, u32[]{:S(2)}, u32[]{:S(2)}) collective-permute-start(bf16[1024,128]{1,0:T(8,128)(2,1)S(1)} %collective-permute-done.34), channel_id=1, source_target_pairs={{0,4},{4,8},{8,12},{12,16},{16,20},{20,24},{24,28},{28,32},{32,36}... | collective-permute-start | bytes 786440 | tf_op jit(solution)/shard_map/ppermute | solution.py:27
  223.9 6.8 %collective-permute-start.59 = (bf16[1024,128]{1,0:T(8,128)(2,1)S(1)}, bf16[1024,128]{1,0:T(8,128)(2,1)S(1)}, u32[]{:S(2)}, u32[]{:S(2)}) collective-permute-start(bf16[1024,128]{1,0:T(8,128)(2,1)S(1)} %collective-permute-done.58), channel_id=1, source_target_pairs={{4,0},{8,4},{12,8},{16,12},{20,16},{24,20},{28,24},{32,28},{36,32}... | collective-permute-start | bytes 786440 | tf_op jit(solution)/shard_map/ppermute | solution.py:29
  225.8 18.3 %collective-permute-start.12 = (bf16[1024,128]{1,0:T(8,128)(2,1)S(1)}, bf16[1024,128]{1,0:T(8,128)(2,1)}, u32[]{:S(2)}, u32[]{:S(2)}) collective-permute-start(bf16[1024,128]{1,0:T(8,128)(2,1)S(1)} %collective-permute-done.11), channel_id=1, source_target_pairs={{4,0},{8,4},{12,8},{16,12},{20,16},{24,20},{28,24},{32,28},{36,32}... | collective-permute-start | bytes 786440 | tf_op jit(solution)/shard_map/ppermute | solution.py:29
  228.9 17.8 %collective-permute-start.43 = (bf16[1024,128]{1,0:T(8,128)(2,1)}, bf16[1024,128]{1,0:T(8,128)(2,1)}, u32[]{:S(2)}, u32[]{:S(2)}) collective-permute-start(bf16[1024,128]{1,0:T(8,128)(2,1)} %collective-permute-done.42), channel_id=1, source_target_pairs={{4,0},{8,4},{12,8},{16,12},{20,16},{24,20},{28,24},{32,28},{36,32}... | collective-permute-start | bytes 786440 | tf_op jit(solution)/shard_map/ppermute | solution.py:29
  229.0 20.7 %collective-permute-start.20 = (bf16[1024,128]{1,0:T(8,128)(2,1)}, bf16[1024,128]{1,0:T(8,128)(2,1)}, u32[]{:S(2)}, u32[]{:S(2)}) collective-permute-start(bf16[1024,128]{1,0:T(8,128)(2,1)} %collective-permute-done.19), channel_id=1, source_target_pairs={{0,4},{4,8},{8,12},{12,16},{16,20},{20,24},{24,28},{28,32},{32,36}... | collective-permute-start | bytes 786440 | tf_op jit(solution)/shard_map/ppermute | solution.py:27
  230.7 18.9 %collective-permute-start.5 = (bf16[1024,128]{1,0:T(8,128)(2,1)}, bf16[1024,128]{1,0:T(8,128)(2,1)}, u32[]{:S(2)}, u32[]{:S(2)}) collective-permute-start(bf16[1024,128]{1,0:T(8,128)(2,1)} %collective-permute-done.4), channel_id=1, source_target_pairs={{0,4},{4,8},{8,12},{12,16},{16,20},{20,24},{24,28},{28,32},{32,36}... | collective-permute-start | bytes 786440 | tf_op jit(solution)/shard_map/ppermute | solution.py:27
  230.7 18.9 %collective-permute-start.36 = (bf16[1024,128]{1,0:T(8,128)(2,1)}, bf16[1024,128]{1,0:T(8,128)(2,1)}, u32[]{:S(2)}, u32[]{:S(2)}) collective-permute-start(bf16[1024,128]{1,0:T(8,128)(2,1)} %collective-permute-done.35), channel_id=1, source_target_pairs={{0,4},{4,8},{8,12},{12,16},{16,20},{20,24},{24,28},{28,32},{32,36}... | collective-permute-start | bytes 786440 | tf_op jit(solution)/shard_map/ppermute | solution.py:27
  244.1 11.7 %collective-permute-start.28 = (bf16[1024,128]{1,0:T(8,128)(2,1)}, bf16[1024,128]{1,0:T(8,128)(2,1)}, u32[]{:S(2)}, u32[]{:S(2)}) collective-permute-start(bf16[1024,128]{1,0:T(8,128)(2,1)} %collective-permute-done.27), channel_id=1, source_target_pairs={{4,0},{8,4},{12,8},{16,12},{20,16},{24,20},{28,24},{32,28},{36,32}... | collective-permute-start | bytes 786440 | tf_op jit(solution)/shard_map/ppermute | solution.py:29
  246.7 9.6 %collective-permute-start.13 = (bf16[1024,128]{1,0:T(8,128)(2,1)}, bf16[1024,128]{1,0:T(8,128)(2,1)}, u32[]{:S(2)}, u32[]{:S(2)}) collective-permute-start(bf16[1024,128]{1,0:T(8,128)(2,1)} %collective-permute-done.12), channel_id=1, source_target_pairs={{4,0},{8,4},{12,8},{16,12},{20,16},{24,20},{28,24},{32,28},{36,32}... | collective-permute-start | bytes 786440 | tf_op jit(solution)/shard_map/ppermute | solution.py:29
  249.6 9.6 %collective-permute-start.21 = (bf16[1024,128]{1,0:T(8,128)(2,1)}, bf16[1024,128]{1,0:T(8,128)(2,1)}, u32[]{:S(2)}, u32[]{:S(2)}) collective-permute-start(bf16[1024,128]{1,0:T(8,128)(2,1)} %collective-permute-done.20), channel_id=1, source_target_pairs={{0,4},{4,8},{8,12},{12,16},{16,20},{20,24},{24,28},{28,32},{32,36}... | collective-permute-start | bytes 786440 | tf_op jit(solution)/shard_map/ppermute | solution.py:27
  249.6 10.1 %collective-permute-start.6 = (bf16[1024,128]{1,0:T(8,128)(2,1)}, bf16[1024,128]{1,0:T(8,128)(2,1)}, u32[]{:S(2)}, u32[]{:S(2)}) collective-permute-start(bf16[1024,128]{1,0:T(8,128)(2,1)} %collective-permute-done.5), channel_id=1, source_target_pairs={{0,4},{4,8},{8,12},{12,16},{16,20},{20,24},{24,28},{28,32},{32,36}... | collective-permute-start | bytes 786440 | tf_op jit(solution)/shard_map/ppermute | solution.py:27
  249.7 11.3 %collective-permute-start.37 = (bf16[1024,128]{1,0:T(8,128)(2,1)}, bf16[1024,128]{1,0:T(8,128)(2,1)}, u32[]{:S(2)}, u32[]{:S(2)}) collective-permute-start(bf16[1024,128]{1,0:T(8,128)(2,1)} %collective-permute-done.36), channel_id=1, source_target_pairs={{0,4},{4,8},{8,12},{12,16},{16,20},{20,24},{24,28},{28,32},{32,36}... | collective-permute-start | bytes 786440 | tf_op jit(solution)/shard_map/ppermute | solution.py:27
  255.6 121.4 %reduce-scatter.9.cloned.1.call-start = ((), (), s32[]{:S(2)}) async-start(), calls=%async_computation.8 | async-start | bytes 2621440 | tf_op jit(solution)/shard_map/reduce_scatter | solution.py:94
  255.7 25.1 %collective-permute-start.44 = (bf16[1024,128]{1,0:T(8,128)(2,1)}, bf16[1024,128]{1,0:T(8,128)(2,1)S(1)}, u32[]{:S(2)}, u32[]{:S(2)}) collective-permute-start(bf16[1024,128]{1,0:T(8,128)(2,1)} %collective-permute-done.43), channel_id=1, source_target_pairs={{4,0},{8,4},{12,8},{16,12},{20,16},{24,20},{28,24},{32,28},{36,32}... | collective-permute-start | bytes 786440 | tf_op jit(solution)/shard_map/ppermute | solution.py:29
  256.2 63.0 %collective-permute-start.29 = (bf16[1024,128]{1,0:T(8,128)(2,1)}, bf16[1024,128]{1,0:T(8,128)(2,1)}, u32[]{:S(2)}, u32[]{:S(2)}) collective-permute-start(bf16[1024,128]{1,0:T(8,128)(2,1)} %collective-permute-done.28), channel_id=1, source_target_pairs={{4,0},{8,4},{12,8},{16,12},{20,16},{24,20},{28,24},{32,28},{36,32}... | collective-permute-start | bytes 786440 | tf_op jit(solution)/shard_map/ppermute | solution.py:29
  259.2 98.2 %collective-permute-start.14 = (bf16[1024,128]{1,0:T(8,128)(2,1)}, bf16[1024,128]{1,0:T(8,128)(2,1)}, u32[]{:S(2)}, u32[]{:S(2)}) collective-permute-start(bf16[1024,128]{1,0:T(8,128)(2,1)} %collective-permute-done.13), channel_id=1, source_target_pairs={{4,0},{8,4},{12,8},{16,12},{20,16},{24,20},{28,24},{32,28},{36,32}... | collective-permute-start | bytes 786440 | tf_op jit(solution)/shard_map/ppermute | solution.py:29
  259.7 40.0 %collective-permute-start.22 = (bf16[1024,128]{1,0:T(8,128)(2,1)}, bf16[1024,128]{1,0:T(8,128)(2,1)}, u32[]{:S(2)}, u32[]{:S(2)}) collective-permute-start(bf16[1024,128]{1,0:T(8,128)(2,1)} %collective-permute-done.21), channel_id=1, source_target_pairs={{0,4},{4,8},{8,12},{12,16},{16,20},{20,24},{24,28},{28,32},{32,36}... | collective-permute-start | bytes 786440 | tf_op jit(solution)/shard_map/ppermute | solution.py:27
  260.9 77.9 %collective-permute-start.7 = (bf16[1024,128]{1,0:T(8,128)(2,1)}, bf16[1024,128]{1,0:T(8,128)(2,1)}, u32[]{:S(2)}, u32[]{:S(2)}) collective-permute-start(bf16[1024,128]{1,0:T(8,128)(2,1)} %collective-permute-done.6), channel_id=1, source_target_pairs={{0,4},{4,8},{8,12},{12,16},{16,20},{20,24},{24,28},{28,32},{32,36}... | collective-permute-start | bytes 786440 | tf_op jit(solution)/shard_map/ppermute | solution.py:27
  299.4 77.6 %reduce-scatter.7.cloned.1.call-start = ((), (), s32[]{:S(2)}) async-start(), calls=%async_computation.7 | async-start | bytes 2621440 | tf_op jit(solution)/shard_map/reduce_scatter | solution.py:94
  338.7 70.5 %reduce-scatter.5.cloned.1.call-start = ((), (), s32[]{:S(2)}) async-start(), calls=%async_computation.6 | async-start | bytes 2621440 | tf_op jit(solution)/shard_map/reduce_scatter | solution.py:94
  (68 other events, 1619.1 us)
Sparse Core Ops, SparseCore 0:
  9.2 64.9 all-gather.1
  255.7 32.0 reduce-scatter.10
  299.5 32.0 reduce-scatter.8
  338.8 32.0 reduce-scatter.6
  377.0 32.0 reduce-scatter.4
